TPU v7x, 256 devices: a whole 4x4x8 slice. The times are simulated.
256 devices in a mesh: rows: 64 (over y, z, core), freq: 4 (over x).
Axes of the slice: x: 4, y: 4, z: 8, core: 2. Of those that a mesh axis runs over, the one named last changes fastest.
Arguments:
- snapshots: bfloat16 [1048576, 512], P('rows', 'freq'), may hold values from -60 to 60
- block_cols: int32 [8192, 3], P('rows'), may hold values from 0 to 8191, as said below
- mass_blocks: bfloat16 [8192, 3, 128, 128], P('rows'), may hold values from -2 to 2
- start_group: float32 [512, 32], P('freq'), may hold values from -6 to 6
- start_merge: float32 [64, 32], replicated, may hold values from -6 to 6
Outputs:
- modes: float32 [32, 1048576], P(None, ('rows', 'freq'))
Inputs may be any that keep to these rules, and one draw needn't show every extreme that they name: block_cols[b, 0] is b; the other entries lie within 2 of b, differ from b, and may repeat near the ends.
All inputs are finite; a program needn't handle non-finite values.
Results may differ from a plain program's by a relative error of at most 0.0003.
Values may be sent and summed in bfloat16 or wider, within the bound.
No kernel may reach another device: no remote copies, remote signals or barrier semaphores. Data moves between devices by JAX's collectives and lax.ppermute only.
A program may use at most 128 MiB of HBM per device.

v0:
```python
import jax
import jax.numpy as jnp
from jax import lax
from jax.sharding import PartitionSpec as P

HB = 2
POWER = 2
HIGHEST = lax.Precision.HIGHEST


def extended_2(block, sides, width):
    for axis, dim in sides:
        count = lax.axis_size(axis)
        forward = [(i, i + 1) for i in range(count - 1)]
        backward = [(target, source) for source, target in forward]
        low = lax.ppermute(
            lax.slice_in_dim(block, block.shape[dim] - width, None, axis=dim), axis, forward
        )
        high = lax.ppermute(lax.slice_in_dim(block, 0, width, axis=dim), axis, backward)
        block = jnp.concatenate([low, block, high], axis=dim)
    return block


def orthonormal(columns_block):
    inner_gram = jnp.dot(columns_block.T, columns_block, precision=HIGHEST)
    lower_factor = jnp.linalg.cholesky(inner_gram)
    return lax.linalg.triangular_solve(
        lower_factor, columns_block, left_side=False, lower=True, transpose_a=True
    )


def subspace(gram_matrix, start_block):
    current = start_block
    for repeat in range(POWER):
        current = orthonormal(jnp.dot(gram_matrix, current, precision=HIGHEST))
    return current


def coefficient_tree(full_gram, start_merge, rank_size, freq_count):
    pairs = freq_count // 2
    width = 2 * rank_size
    blocks = jnp.stack(
        [full_gram[p * width : (p + 1) * width, p * width : (p + 1) * width] for p in range(pairs)]
    )
    pair_weights = jax.vmap(subspace, in_axes=(0, None))(blocks, start_merge)
    zero = jnp.zeros((width, rank_size), jnp.float32)
    coefficients = []
    for p in range(pairs):
        parts = [zero] * pairs
        parts[p] = pair_weights[p]
        coefficients.append(jnp.concatenate(parts, axis=0))
    while len(coefficients) > 1:
        merged = []
        for position in range(0, len(coefficients), 2):
            joined = jnp.concatenate([coefficients[position], coefficients[position + 1]], axis=1)
            pair_gram = jnp.dot(
                joined.T, jnp.dot(full_gram, joined, precision=HIGHEST), precision=HIGHEST
            )
            merged.append(jnp.dot(joined, subspace(pair_gram, start_merge), precision=HIGHEST))
        coefficients = merged
    return coefficients[0]


def shards(snapshots, block_cols, mass_blocks, start_group, start_merge):
    block_size = mass_blocks.shape[2]
    local_blocks = block_cols.shape[0]
    local_cols = snapshots.shape[1]
    total_rows = lax.axis_size("rows") * snapshots.shape[0]
    extended = extended_2(snapshots, (("rows", 0),), HB * block_size)
    tile_stack = extended.reshape(local_blocks + 2 * HB, block_size, local_cols)
    local_index = block_cols - lax.axis_index("rows") * local_blocks + HB
    picked = tile_stack[local_index]
    weighted = jnp.einsum("bkij,bkjc->bic", mass_blocks, picked, preferred_element_type=jnp.float32)
    weighted = weighted.reshape(local_blocks * block_size, local_cols)
    local_gram = jnp.dot(weighted.T, weighted, precision=HIGHEST)
    group_gram = lax.psum(local_gram, "rows") / total_rows
    weights = subspace(group_gram, start_group)
    modes = lax.dot_general(weights, weighted, (((0,), (1,)), ((), ())), precision=HIGHEST)
    rank_size = modes.shape[0]
    freq_count = lax.axis_size("freq")
    quarter = lax.all_to_all(modes, "freq", 1, 0, tiled=True)
    full_gram = (
        lax.psum(jnp.dot(quarter, quarter.T, precision=HIGHEST), ("rows", "freq")) / total_rows
    )
    combined = coefficient_tree(full_gram, start_merge, rank_size, freq_count)
    result = jnp.dot(combined.T, quarter, precision=HIGHEST)
    return result


def solution(mesh):
    in_specs = (
        P("rows", "freq"),
        P("rows", None),
        P("rows", None, None, None),
        P("freq", None),
        P(),
    )
    out_specs = P(None, ("rows", "freq"))
    return jax.shard_map(shards, mesh=mesh, in_specs=in_specs, out_specs=out_specs, check_vma=False)
```

profile of v0, /device:TPU:1, one launch (start us, length us, event | category | flops | bytes accessed | tf_op | source)
XLA Modules:
  0.0 596.8 jit_solution(17205891390755514347)
XLA Ops:
  7.4 4.9 collective-permute-start
  15.3 2.6 collective-permute-done.1
  18.0 10.8 %pad_maximum_fusion = bf16[16896,128]{1,0:T(8,128)(2,1)} fusion(bf16[256,128]{1,0:T(8,128)(2,1)S(1)} %collective-permute-done.1, bf16[16384,128]{1,0:T(8,128)(2,1)} %param.13, bf16[256,128]{1,0:T(8,128)(2,1)S(1)} %collective-permute-done), kind=kLoop, calls=%fused_computation.3 | loop fusion | flops 12976128 | bytes 8650752 | tf_op jit(solution)/shard_map/concatenate | solution.py:20
  28.7 13.6 %gather_fusion = bf16[384,128,128]{2,1,0:T(8,128)(2,1)} fusion(bf16[132,128,128]{2,1,0:T(8,128)(2,1)} %bitcast.133, s32[1024]{0:T(1024)S(1)} %pad_clamp_fusion), kind=kCustom, calls=%fused_computation | custom fusion | bytes 25167360 | tf_op jit(solution)/shard_map/gather | solution.py:72
  42.3 14.8 %fusion.62 = f32[128,128,128,1]{1,2,3,0:T(8,128)} fusion(bf16[128,3,128,128]{3,2,1,0:T(8,128)(2,1)} %param.15, bf16[128,3,128,128]{3,2,1,0:T(8,128)(2,1)} %bitcast.132), kind=kOutput, calls=%fused_computation.103 | convolution fusion | flops 1610612736 | bytes 33554432 | tf_op jit(solution)/shard_map/bkij,bkjc->bic/dot_general | solution.py:73
  57.1 17.6 %fusion.2 = f32[128,128]{1,0:T(8,128)} fusion(f32[128,128,128,1]{1,2,3,0:T(8,128)} %fusion.62), kind=kOutput, calls=%fused_computation.4 | convolution fusion | flops 3221225472 | bytes 8454144 | tf_op jit(solution)/shard_map/dot_general | solution.py:75
  74.7 173.3 %all-reduce.5.cloned.1.call-done = f32[128,128]{1,0:T(8,128)} async-done(((f32[128,128]{1,0:T(8,128)}), f32[128,128]{1,0:T(8,128)}) %all-reduce.5.cloned.1.call-update) | async-done | bytes 65552 | tf_op jit(solution)/shard_map/psum | solution.py:76
  249.3 2.9 cholesky.117
  253.6 2.4 custom-call.18
  257.6 2.9 cholesky.128
  261.8 2.4 custom-call.19
  264.5 13.0 %fusion.53 = f32[32,4,4096]{2,0,1:T(8,128)} fusion(f32[128,32,1]{0,1,2:T(8,128)S(1)} %convolution_bitcast_fusion.4, f32[4,4096,128]{2,1,0:T(8,128)} %bitcast.131), kind=kOutput, calls=%fused_computation.94 | convolution fusion | flops 805306368 | bytes 10502144 | tf_op jit(solution)/shard_map/dot_general | solution.py:78
  277.5 4.0 all-to-all-start
  281.5 25.8 %all-to-all-done = f32[32,4,4096]{2,0,1:T(8,128)S(1)} async-done(((f32[32,4,4096]{2,0,1:T(8,128)}), f32[32,4,4096]{2,0,1:T(8,128)S(1)}, u32[]{:S(2)}, u32[]{:S(2)}) %all-to-all-start) | async-done | bytes 2097184 | tf_op jit(solution)/shard_map/all_to_all | solution.py:81
  307.2 2.4 fusion.54
  309.7 237.2 %all-reduce.7.cloned.1.call-done = f32[128,128]{1,0:T(8,128)} async-done(((f32[128,128]{1,0:T(8,128)}), f32[128,128]{1,0:T(8,128)}) %all-reduce.7.cloned.1.call-update) | async-done | bytes 65552 | tf_op jit(solution)/shard_map/psum | solution.py:83
  548.4 6.1 %custom-call.20 = f32[2,32,32]{2,1,0:T(8,128)S(1)} custom-call(f32[2,32,32]{2,1,0:T(8,128)S(1)} %fusion.14), custom_call_target="Cholesky" | custom-call | tf_op jit(solution)/shard_map/vmap(jit(cholesky))/cholesky | solution.py:26
  554.8 4.9 custom-call.21
  560.5 5.9 custom-call.22
  566.6 4.9 custom-call.23
  573.5 2.9 cholesky.161
  577.8 2.4 custom-call.24
  580.9 2.9 cholesky.172
  585.1 2.4 custom-call.25
  (72 shorter events, 19.9 us)
Async XLA Ops:
  6.5 541.3 %copy-start = (f32[64,32]{0,1:T(8,128)S(1)}, f32[64,32]{0,1:T(8,128)}, u32[]{:S(2)}) copy-start(f32[64,32]{0,1:T(8,128)} %param.17) | copy-start | bytes 24580
  6.5 241.5 %all-reduce.5.cloned.1.call-start = ((), (), s32[]{:S(2)}) async-start(), calls=%async_computation.1 | async-start | bytes 131072 | tf_op jit(solution)/shard_map/psum | solution.py:76
  7.4 7.9 %collective-permute-start = (bf16[256,128]{1,0:T(8,128)(2,1)S(1)}, bf16[256,128]{1,0:T(8,128)(2,1)S(1)}, u32[]{:S(2)}, u32[]{:S(2)}) collective-permute-start(bf16[256,128]{1,0:T(8,128)(2,1)S(1)} %get-tuple-element.6), channel_id=1, source_target_pairs={{0,4},{4,8},{8,12},{12,16},{16,20},{20,24},{24,28},{28,32},{32,36}... | collective-permute-start | bytes 196616 | tf_op jit(solution)/shard_map/ppermute | solution.py:16
  12.4 5.6 collective-permute-start.1
  57.1 191.0 %copy-start.1 = (f32[128,32]{0,1:T(8,128)S(1)}, f32[128,32]{0,1:T(8,128)}, u32[]{:S(2)}) copy-start(f32[128,32]{0,1:T(8,128)} %param.16) | copy-start | bytes 49156
  277.5 29.7 %all-to-all-start = ((f32[32,4,4096]{2,0,1:T(8,128)}), f32[32,4,4096]{2,0,1:T(8,128)S(1)}, u32[]{:S(2)}, u32[]{:S(2)}) async-start(f32[32,4,4096]{2,0,1:T(8,128)} %fusion.53), calls=%async_computation | async-start | bytes 4194304 | tf_op jit(solution)/shard_map/all_to_all | solution.py:81
  281.5 265.5 %all-reduce.7.cloned.1.call-start = ((), (), s32[]{:S(2)}) async-start(), calls=%async_computation.2 | async-start | bytes 131072 | tf_op jit(solution)/shard_map/psum | solution.py:83
Sparse Core Ops, SparseCore 0:
  74.8 173.1 all-reduce.4
  309.8 237.0 all-reduce.6
where the time goes:
time: 597 us
  waiting for transfers between devices  439 us (74%)
  other arithmetic  61.4 us (10%)
  matrix products  56.6 us (9%)
  local copies, waits for them, and re-layouts  15.3 us (3%)
  between operations  13.7 us (2%)
  starting transfers between devices  10.8 us (2%)
    psum x1, waiting for transfers between devices, shards(): lax.psum(jnp.dot(quarter, quarter.T, precision=HIGHEST), ('rows', 'freq'))  237 us
    psum x1, waiting for transfers between devices, shards(): group_gram = lax.psum(local_gram, 'rows') / total_rows  173 us
    another operation x19, other arithmetic, orthonormal(): lower_factor = jnp.linalg.cholesky(inner_gram)  26.7 us
    all_to_all x1, waiting for transfers between devices, shards(): quarter = lax.all_to_all(modes, 'freq', 1, 0, tiled=True)  25.8 us
    another operation x13, other arithmetic, orthonormal(): lax.linalg.triangular_solve(lower_factor, columns_block, left_side=False,...  22.3 us
    dot_general x1, matrix products, shards(): local_gram = jnp.dot(weighted.T, weighted, precision=HIGHEST)  17.6 us
    dot_general x1, matrix products, shards(): jnp.einsum('bkij,bkjc->bic', mass_blocks, picked, preferred_element_type=...  14.8 us
    gather x1, local copies, waits for them, and re-layouts, shards(): picked = tile_stack[local_index]  13.6 us
  transfers between devices with their start and end apart: 5, of which 4 were waited for; matrix products, arithmetic and copies ran while one was open for 0% of the time, Pallas kernels for 0%

commit v1 on v0

--- a/solution.py
+++ b/solution.py
@@ -78,7 +78,9 @@
     modes = lax.dot_general(weights, weighted, (((0,), (1,)), ((), ())), precision=HIGHEST)
     rank_size = modes.shape[0]
     freq_count = lax.axis_size("freq")
-    quarter = lax.all_to_all(modes, "freq", 1, 0, tiled=True)
+    quarter = jnp.concatenate(
+        lax.all_to_all(jnp.stack(jnp.split(modes, lax.axis_size("freq"), 1), 0), "freq", 0, 0), 0
+    )
     full_gram = (
         lax.psum(jnp.dot(quarter, quarter.T, precision=HIGHEST), ("rows", "freq")) / total_rows
     )

time: 597 us -> 597 us (level)
  no operation moved by 1% of the time
where the time goes in v1:
time: 597 us; the launch traced here: 596 us
  waiting for transfers between devices  439 us (74%)
  other arithmetic  62.7 us (11%)
  matrix products  54.6 us (9%)
  local copies, waits for them, and re-layouts  15.5 us (3%)
  between operations  13.7 us (2%)
  starting transfers between devices  10.8 us (2%)
    psum x1, waiting for transfers between devices, shards(): lax.psum(jnp.dot(quarter, quarter.T, precision=HIGHEST), ('rows', 'freq'))  237 us
    psum x1, waiting for transfers between devices, shards(): group_gram = lax.psum(local_gram, 'rows') / total_rows  173 us
    another operation x19, other arithmetic, orthonormal(): lower_factor = jnp.linalg.cholesky(inner_gram)  26.4 us
    all_to_all x1, waiting for transfers between devices, shards(): lax.all_to_all(jnp.stack(jnp.split(modes, lax.axis_size('freq'), 1), 0),...  25.8 us
    another operation x13, other arithmetic, orthonormal(): lax.linalg.triangular_solve(lower_factor, columns_block, left_side=False,...  22.3 us
    dot_general x1, matrix products, shards(): local_gram = jnp.dot(weighted.T, weighted, precision=HIGHEST)  17.6 us
    dot_general x1, matrix products, shards(): jnp.einsum('bkij,bkjc->bic', mass_blocks, picked, preferred_element_type=...  14.8 us
    gather x1, local copies, waits for them, and re-layouts, shards(): picked = tile_stack[local_index]  13.6 us
  transfers between devices with their start and end apart: 5, of which 4 were waited for; matrix products, arithmetic and copies ran while one was open for 0% of the time, Pallas kernels for 0%

profile of v1, /device:TPU:1, one launch (start us, length us, event | category | flops | bytes accessed | tf_op | source)
XLA Modules:
  0.0 596.1 jit_solution(16974677134353535647)
XLA Ops:
  7.4 4.9 collective-permute-start
  15.3 2.6 collective-permute-done.1
  18.0 10.8 %pad_maximum_fusion = bf16[16896,128]{1,0:T(8,128)(2,1)} fusion(bf16[256,128]{1,0:T(8,128)(2,1)S(1)} %collective-permute-done.1, bf16[16384,128]{1,0:T(8,128)(2,1)} %param.13, bf16[256,128]{1,0:T(8,128)(2,1)S(1)} %collective-permute-done), kind=kLoop, calls=%fused_computation.3 | loop fusion | flops 12976128 | bytes 8650752 | tf_op jit(solution)/shard_map/concatenate | solution.py:20
  28.7 13.6 %gather_fusion = bf16[384,128,128]{2,1,0:T(8,128)(2,1)} fusion(bf16[132,128,128]{2,1,0:T(8,128)(2,1)} %bitcast.137, s32[1024]{0:T(1024)S(1)} %pad_clamp_fusion), kind=kCustom, calls=%fused_computation | custom fusion | bytes 25167360 | tf_op jit(solution)/shard_map/gather | solution.py:72
  42.3 14.8 %fusion.62 = f32[128,128,128,1]{1,2,3,0:T(8,128)} fusion(bf16[128,3,128,128]{3,2,1,0:T(8,128)(2,1)} %param.15, bf16[128,3,128,128]{3,2,1,0:T(8,128)(2,1)} %bitcast.136), kind=kOutput, calls=%fused_computation.108 | convolution fusion | flops 1610612736 | bytes 33554432 | tf_op jit(solution)/shard_map/bkij,bkjc->bic/dot_general | solution.py:73
  57.1 17.6 %fusion.2 = f32[128,128]{1,0:T(8,128)} fusion(f32[128,128,128,1]{1,2,3,0:T(8,128)} %fusion.62), kind=kOutput, calls=%fused_computation.5 | convolution fusion | flops 3221225472 | bytes 8454144 | tf_op jit(solution)/shard_map/dot_general | solution.py:75
  74.7 173.3 %all-reduce.5.cloned.1.call-done = f32[128,128]{1,0:T(8,128)} async-done(((f32[128,128]{1,0:T(8,128)}), f32[128,128]{1,0:T(8,128)}) %all-reduce.5.cloned.1.call-update) | async-done | bytes 65552 | tf_op jit(solution)/shard_map/psum | solution.py:76
  249.3 2.9 cholesky.117
  253.6 2.4 custom-call.18
  257.6 2.9 cholesky.128
  261.8 2.4 custom-call.19
  264.5 10.9 %fusion.53 = f32[32,16384]{1,0:T(8,128)S(1)} fusion(f32[128,32]{0,1:T(8,128)S(1)} %convolution_bitcast_fusion.4, f32[16384,128]{1,0:T(8,128)} %bitcast.135), kind=kOutput, calls=%fused_computation.99 | convolution fusion | flops 805306368 | bytes 10502144 | tf_op jit(solution)/shard_map/dot_general | solution.py:78
  277.1 4.0 all-to-all-start
  281.1 25.8 %all-to-all-done = f32[4,32,4096]{2,1,0:T(8,128)S(1)} async-done(((f32[4,32,4096]{2,1,0:T(8,128)}), f32[4,32,4096]{2,1,0:T(8,128)S(1)}, u32[]{:S(2)}, u32[]{:S(2)}) %all-to-all-start) | async-done | bytes 2097184 | tf_op jit(solution)/shard_map/all_to_all | solution.py:82
  306.8 2.4 fusion.54
  309.3 237.2 %all-reduce.7.cloned.1.call-done = f32[128,128]{1,0:T(8,128)} async-done(((f32[128,128]{1,0:T(8,128)}), f32[128,128]{1,0:T(8,128)}) %all-reduce.7.cloned.1.call-update) | async-done | bytes 65552 | tf_op jit(solution)/shard_map/psum | solution.py:85
  548.0 5.9 custom-call.20
  554.1 4.9 custom-call.21
  559.8 5.9 custom-call.22
  565.9 4.9 custom-call.23
  572.8 2.9 cholesky.161
  577.1 2.4 custom-call.24
  580.2 2.9 cholesky.172
  584.4 2.4 custom-call.25
  (74 shorter events, 21.6 us)
Async XLA Ops:
  6.5 540.9 %copy-start = (f32[64,32]{0,1:T(8,128)S(1)}, f32[64,32]{0,1:T(8,128)}, u32[]{:S(2)}) copy-start(f32[64,32]{0,1:T(8,128)} %param.17) | copy-start | bytes 24580
  6.5 241.5 %all-reduce.5.cloned.1.call-start = ((), (), s32[]{:S(2)}) async-start(), calls=%async_computation.1 | async-start | bytes 131072 | tf_op jit(solution)/shard_map/psum | solution.py:76
  7.4 7.9 %collective-permute-start = (bf16[256,128]{1,0:T(8,128)(2,1)S(1)}, bf16[256,128]{1,0:T(8,128)(2,1)S(1)}, u32[]{:S(2)}, u32[]{:S(2)}) collective-permute-start(bf16[256,128]{1,0:T(8,128)(2,1)S(1)} %get-tuple-element.6), channel_id=1, source_target_pairs={{0,4},{4,8},{8,12},{12,16},{16,20},{20,24},{24,28},{28,32},{32,36}... | collective-permute-start | bytes 196616 | tf_op jit(solution)/shard_map/ppermute | solution.py:16
  12.4 5.6 collective-permute-start.1
  57.1 191.0 %copy-start.1 = (f32[128,32]{0,1:T(8,128)S(1)}, f32[128,32]{0,1:T(8,128)}, u32[]{:S(2)}) copy-start(f32[128,32]{0,1:T(8,128)} %param.16) | copy-start | bytes 49156
  277.1 29.7 %all-to-all-start = ((f32[4,32,4096]{2,1,0:T(8,128)}), f32[4,32,4096]{2,1,0:T(8,128)S(1)}, u32[]{:S(2)}, u32[]{:S(2)}) async-start(f32[4,32,4096]{2,1,0:T(8,128)} %pad_maximum_fusion.1), calls=%async_computation | async-start | bytes 4194304 | tf_op jit(solution)/shard_map/all_to_all | solution.py:82
  281.0 265.4 %all-reduce.7.cloned.1.call-start = ((), (), s32[]{:S(2)}) async-start(), calls=%async_computation.2 | async-start | bytes 131072 | tf_op jit(solution)/shard_map/psum | solution.py:85
Sparse Core Ops, SparseCore 0:
  74.8 173.1 all-reduce.4
  309.4 237.0 all-reduce.6
